TPU v7x, 256 devices: a whole 4x4x8 slice. The times are simulated.
256 devices in a mesh: node: 8 (over z_lo, core), drow: 4 (over x), dcol: 8 (over z_hi, y).
Axes of the slice: x: 4, y: 4, z: 8 (z_hi: 2, z_lo: 4; z = z_hi * 4 + z_lo), core: 2. Of those that a mesh axis runs over, the one named last changes fastest.
Arguments:
- freq_resp: bfloat16 [2, 8, 4096, 8192], P(None, None, ('drow', 'dcol'), 'node'), may hold values from -0.0625 to 0.0625
- node_coords: int32 [2, 8192], P(None, 'node'), may hold values from 0 to 1023
- heading_steps: int32 [2, 512], replicated, may hold values from -8 to 8
- spectral_weights: int32 [8, 512], replicated, may hold values from 1 to 64
Outputs:
- cross_spectra: float32 [2, 8, 4, 1024, 4096], P(None, None, 'drow', 'node', 'dcol')
All inputs are finite; a program needn't handle non-finite values.
Results may differ from a plain program's by a relative error of at most 0.0038.
Values may be sent and summed in bfloat16 or wider, within the bound.
No kernel may reach another device: no remote copies, remote signals or barrier semaphores. Data moves between devices by JAX's collectives and lax.ppermute only.
A program may use at most 128 MiB of HBM per device.

v0:
```python
import math
import jax
import jax.numpy as jnp
from jax import lax
from jax.sharding import PartitionSpec as P

DIRS = 512
FREQS = 8
GRID = 1024


def excitation(coords, heading_steps, spectral_weights):
    freq_index = (jnp.arange(FREQS, dtype=jnp.int32) + 1)[:, None, None]
    project = (
        coords[0][:, None] * heading_steps[0][None, :]
        + coords[1][:, None] * heading_steps[1][None, :]
    )
    turn_count = jnp.mod(freq_index * project[None], GRID)
    phase_angle = turn_count.astype(jnp.float32) * (2.0 * math.pi / GRID)
    spread = jnp.sqrt(spectral_weights.astype(jnp.float32) / (64.0 * DIRS))[:, None, :]
    load_re = (spread * jnp.cos(phase_angle)).astype(jnp.bfloat16)
    load_im = (-spread * jnp.sin(phase_angle)).astype(jnp.bfloat16)
    return (load_re, load_im)


def local(freq_resp, node_coords, heading_steps, spectral_weights):
    load_re, load_im = excitation(node_coords, heading_steps, spectral_weights)
    right_re = jnp.concatenate([load_re, load_im], axis=1)
    right_im = jnp.concatenate([load_im, load_re], axis=1)
    left_re = jnp.concatenate([freq_resp[0], -freq_resp[1]], axis=2)
    left_im = jnp.concatenate([freq_resp[0], freq_resp[1]], axis=2)
    amp_re = jnp.einsum("fkn,fnd->kfd", left_re, right_re, preferred_element_type=jnp.float32)
    amp_im = jnp.einsum("fkn,fnd->kfd", left_im, right_im, preferred_element_type=jnp.float32)
    partial_amp = jnp.stack([amp_re, amp_im], axis=1)
    by_dirs = lax.psum_scatter(partial_amp, "node", scatter_dimension=3, tiled=True).astype(
        jnp.bfloat16
    )
    amplitudes = lax.all_to_all(by_dirs, "node", split_axis=0, concat_axis=3, tiled=True)
    colset = lax.all_gather(amplitudes[None], ("node", "drow"), axis=0, tiled=True)
    col_cat = jnp.concatenate([colset[:, :, 0], colset[:, :, 1]], axis=-1)
    row_piece = lax.all_gather(amplitudes, "dcol", axis=0, tiled=True)
    lead_re = jnp.concatenate([row_piece[:, 0], row_piece[:, 1]], axis=-1)
    lead_im = jnp.concatenate([row_piece[:, 1], -row_piece[:, 0]], axis=-1)
    spec_re = jnp.einsum("kfe,gsfe->fkgs", lead_re, col_cat, preferred_element_type=jnp.float32)
    spec_im = jnp.einsum("kfe,gsfe->fkgs", lead_im, col_cat, preferred_element_type=jnp.float32)
    col_width = spec_re.shape[2] * spec_re.shape[3]
    spec_re = spec_re.reshape(spec_re.shape[0], spec_re.shape[1], col_width)
    spec_im = spec_im.reshape(spec_im.shape[0], spec_im.shape[1], col_width)
    return jnp.stack([spec_re, spec_im], axis=0)[:, :, None]


def solution(mesh):
    placed = (P(None, None, ("drow", "dcol"), "node"), P(None, "node"), P(), P())
    return jax.shard_map(
        local,
        mesh=mesh,
        in_specs=placed,
        out_specs=P(None, None, "drow", "node", "dcol"),
        check_vma=False,
    )
```

profile of v0, /device:TPU:1, one launch (start us, length us, event | category | flops | bytes accessed | tf_op | source)
XLA Modules:
  0.0 401.3 jit_solution(3338056714122250045)
XLA Ops:
  6.5 0.0 reduce-scatter.2.cloned.1.call-start
  6.5 0.0 copy-start
  6.5 0.0 copy-start.4
  6.5 2.8 slice_bitcast_fusion
  9.4 0.6 copy-done
  10.0 0.0 copy-start.5
  10.0 0.0 copy-start.3
  10.0 0.1 fusion.33
  10.1 0.0 copy-done.4
  10.2 0.5 copy-done.5
  10.7 0.0 copy-done.3
  10.7 0.4 multiply_add_fusion
  11.1 71.0 %multiply_convert_fusion = (bf16[8,1024,512]{1,2,0:T(8,128)(2,1)}, bf16[8,1024,512]{1,2,0:T(8,128)(2,1)}) fusion(f32[8,512]{1,0:T(8,128)S(1)} %get-tuple-element.13, s32[1024,512]{0,1:T(8,128)S(1)} %multiply_add_fusion, s32[8]{0:T(128)S(1)} %iota_add_fusion, f32[8,512]{1,0:T(8,128)S(1)} %get-tuple-element.14), kind=kLoop, calls=%fused_computation.16 | loop fusion | flops 75497472 | bytes 18907168 | tf_op jit(solution)/shard_map/convert_element_type | solution.py:22
  82.1 9.2 %fusion.21 = f32[128,1,8,512]{0,3,2,1:T(8,128)} fusion(bf16[8,128,1024]{2,1,0:T(8,128)(2,1)S(1)} %get-tuple-element.8, bf16[8,128,1024]{2,1,0:T(8,128)(2,1)S(1)} %get-tuple-element.7, bf16[8,1024,512]{1,2,0:T(8,128)(2,1)} %get-tuple-element.10, bf16[8,1024,512]{1,2,0:T(8,128)(2,1)} %get-tuple-element.9), kind=kOutput, calls=%fused_computation.40 | convolution fusion | flops 2189426688 | bytes 23068672 | tf_op jit(solution)/shard_map/fkn,fnd->kfd/dot_general | solution.py:33
  91.3 0.0 copy-start.2
  91.3 9.3 %fusion.24 = f32[128,1,8,512]{0,3,2,1:T(8,128)} fusion(bf16[8,128,1024]{2,1,0:T(8,128)(2,1)S(1)} %get-tuple-element.8, bf16[8,128,1024]{2,1,0:T(8,128)(2,1)S(1)} %fusion.33, bf16[8,1024,512]{1,2,0:T(8,128)(2,1)} %get-tuple-element.9, bf16[8,1024,512]{1,2,0:T(8,128)(2,1)} %get-tuple-element.10), kind=kOutput, calls=%fused_computation.41 | convolution fusion | flops 2189426688 | bytes 23068672 | tf_op jit(solution)/shard_map/fkn,fnd->kfd/dot_general | solution.py:32
  100.6 0.0 copy-done.2
  100.6 3.9 pad_maximum_fusion.5
  104.6 0.0 reduce-scatter.2.cloned.1.call-update
  104.6 0.0 all-gather.3.cloned.1.call-start
  104.6 56.8 %reduce-scatter.2.cloned.1.call-done = f32[128,2,8,64]{0,3,2,1:T(8,128)} async-done(((f32[128,2,8,512]{0,3,2,1:T(8,128)}), f32[128,2,8,64]{0,3,2,1:T(8,128)}) %reduce-scatter.2.cloned.1.call-update) | async-done | bytes 524304 | tf_op jit(solution)/shard_map/reduce_scatter | solution.py:35
  161.4 1.1 convert_element_type.19
  162.5 0.4 copy.14
  162.9 0.4 reshape.71
  163.3 14.2 %all_to_all.18 = bf16[8,2,8192]{2,1,0:T(2,128)(2,1)S(1)} all-to-all(bf16[8,2,8192]{2,1,0:T(2,128)(2,1)S(1)} %reshape.71), channel_id=1, replica_groups=mesh['node'=8,'drow'=4,'dcol'=8] {'node'}, dimensions={0} | all-to-all | bytes 524288 | tf_op jit(solution)/shard_map/all_to_all | solution.py:38
  177.5 0.3 reshape.72
  177.9 0.3 copy.15
  178.2 1.0 all_to_all.16
  179.2 0.0 all-gather.3.cloned.1.call-update
  179.3 0.0 all-gather.5.cloned.1.call-start
  179.3 0.6 copy.16
  179.9 1.0 broadcast_in_dim.4
  180.9 0.0 all-gather.5.cloned.1.call-update
  181.0 73.6 %all-gather.3.cloned.1.call-done = bf16[128,2,8,512]{3,0,2,1:T(8,128)(2,1)} async-done(((bf16[16,2,8,512]{3,0,2,1:T(8,128)(2,1)}), bf16[128,2,8,512]{3,0,2,1:T(8,128)(2,1)}) %all-gather.3.cloned.1.call-update) | async-done | bytes 2097168 | tf_op jit(solution)/shard_map/all_gather | solution.py:41
  254.5 1.3 fusion.32
  255.8 1.7 slice_bitcast_fusion.3
  257.6 91.3 %all-gather.5.cloned.1.call-done = bf16[32,16,2,8,512]{4,3,2,1,0:T(8,128)(2,1)} async-done(((bf16[1,16,2,8,512]{4,3,2,1,0:T(8,128)(2,1)}), bf16[32,16,2,8,512]{4,3,2,1,0:T(8,128)(2,1)}) %all-gather.5.cloned.1.call-update) | async-done | bytes 8388624 | tf_op jit(solution)/shard_map/all_gather | solution.py:39
  348.9 3.8 fusion.34
  352.7 11.6 %copy_bitcast_fusion = (bf16[32,16,8,512]{3,0,1,2:T(8,128)(2,1)}, bf16[32,16,8,512]{3,0,1,2:T(8,128)(2,1)}) fusion(bf16[32,16,1,8,512]{4,3,2,1,0:T(8,128)(2,1)S(1)} %get-tuple-element.6, bf16[32,16,1,8,512]{4,3,2,1,0:T(8,128)(2,1)S(1)} %get-tuple-element.5), kind=kLoop, calls=%fused_computation.29 | loop fusion | bytes 16777216 | tf_op jit(solution)/shard_map/squeeze | solution.py:40
  364.2 8.2 %pad_maximum_fusion = bf16[32,16,8,1024]{3,0,1,2:T(8,128)(2,1)} fusion(bf16[32,16,8,512]{3,0,1,2:T(8,128)(2,1)} %get-tuple-element.19, bf16[32,16,8,512]{3,0,1,2:T(8,128)(2,1)} %get-tuple-element.20), kind=kLoop, calls=%fused_computation.18 | loop fusion | flops 16777216 | bytes 16777216 | tf_op jit(solution)/shard_map/concatenate | solution.py:40
  372.4 0.0 copy-start.1
  372.5 10.0 %fusion.13 = f32[8,128,32,16]{1,3,2,0:T(8,128)S(1)} fusion(bf16[32,16,8,1024]{3,0,1,2:T(8,128)(2,1)} %pad_maximum_fusion, bf16[128,8,512]{2,0,1:T(8,128)(2,1)S(1)} %get-tuple-element.12, bf16[128,8,512]{2,0,1:T(8,128)(2,1)S(1)} %get-tuple-element.11), kind=kOutput, calls=%fused_computation.21 | convolution fusion | flops 1077936128 | bytes 12582912 | tf_op jit(solution)/shard_map/kfe,gsfe->fkgs/dot_general | solution.py:44
  382.5 0.0 copy-done.1
  382.5 4.6 %fusion.11 = f32[8,128,32,16]{1,3,2,0:T(8,128)S(1)} fusion(bf16[32,16,8,1024]{3,0,1,2:T(8,128)(2,1)S(1)} %copy-done.1, bf16[128,8,512]{2,0,1:T(8,128)(2,1)S(1)} %fusion.32, bf16[128,8,512]{2,0,1:T(8,128)(2,1)S(1)} %get-tuple-element.12), kind=kOutput, calls=%fused_computation.19 | convolution fusion | flops 1077936128 | bytes 12582912 | tf_op jit(solution)/shard_map/kfe,gsfe->fkgs/dot_general | solution.py:45
  387.1 2.2 maximum_bitcast_fusion
  389.4 5.3 %copy.21 = f32[2,8,1,128,512]{4,3,2,1,0:T(8,128)} copy(f32[2,8,1,128,512]{3,4,1,0,2:T(8,128)} %maximum_bitcast_fusion) | data formatting | bytes 8388608 | tf_op jit(solution)/shard_map/broadcast_in_dim | solution.py:49
  (4 shorter events, 0.0 us)
Async XLA Ops:
  6.5 154.9 %reduce-scatter.2.cloned.1.call-start = ((), (), s32[]{:S(2)}) async-start(), calls=%async_computation.2 | async-start | bytes 4718592 | tf_op jit(solution)/shard_map/reduce_scatter | solution.py:35
  6.5 3.4 copy-start
  6.5 3.6 copy-start.4
  10.0 0.7 copy-start.5
  10.0 0.7 copy-start.3
  91.3 9.3 %copy-start.2 = (f32[128,1,8,512]{0,3,2,1:T(8,128)S(1)}, f32[128,1,8,512]{0,3,2,1:T(8,128)}, u32[]{:S(2)}) copy-start(f32[128,1,8,512]{0,3,2,1:T(8,128)} %fusion.21) | copy-start | bytes 6291460
  104.6 150.0 %all-gather.3.cloned.1.call-start = ((), (), s32[]{:S(2)}) async-start(), calls=%async_computation.3 | async-start | bytes 2359296 | tf_op jit(solution)/shard_map/all_gather | solution.py:41
  179.3 169.6 %all-gather.5.cloned.1.call-start = ((), (), s32[]{:S(2)}) async-start(), calls=%async_computation.4 | async-start | bytes 8650752 | tf_op jit(solution)/shard_map/all_gather | solution.py:39
  372.4 10.0 %copy-start.1 = (bf16[32,16,8,1024]{3,0,1,2:T(8,128)(2,1)S(1)}, bf16[32,16,8,1024]{3,0,1,2:T(8,128)(2,1)}, u32[]{:S(2)}) copy-start(bf16[32,16,8,1024]{3,0,1,2:T(8,128)(2,1)} %pad_maximum_fusion) | copy-start | bytes 25165828
Sparse Core Ops, SparseCore 0:
  104.7 56.6 reduce-scatter.1
  179.4 75.1 all-gather.2
  256.4 92.4 all-gather.4
where the time goes:
time: 402 us; the launch traced here: 401 us
  waiting for transfers between devices  222 us (55%)
  other arithmetic  88.3 us (22%)
  matrix products  33.2 us (8%)
  local copies, waits for them, and re-layouts  30.6 us (8%)
  blocking collectives  14.2 us (4%)
  between operations  13.2 us (3%)
    all_gather x1, waiting for transfers between devices, local(): lax.all_gather(amplitudes[None], ('node', 'drow'), axis=0, tiled=True)  91.3 us
    all_gather x1, waiting for transfers between devices, local(): row_piece = lax.all_gather(amplitudes, 'dcol', axis=0, tiled=True)  73.6 us
    convert_element_type x1, other arithmetic, excitation(): load_im = (-spread * jnp.sin(phase_angle)).astype(jnp.bfloat16)  71 us
    reduce_scatter x1, waiting for transfers between devices, local(): lax.psum_scatter(partial_amp, 'node', scatter_dimension=3, tiled=True)  56.8 us
    all_to_all x1, blocking collectives, local(): lax.all_to_all(by_dirs, 'node', split_axis=0, concat_axis=3, tiled=True)  14.2 us
    squeeze x1, local copies, waits for them, and re-layouts, local(): col_cat = jnp.concatenate([colset[:, :, 0], colset[:, :, 1]], axis=-1)  11.6 us
    dot_general x1, matrix products, local(): jnp.einsum('kfe,gsfe->fkgs', lead_re, col_cat, preferred_element_type=jnp...  10 us
    dot_general x1, matrix products, local(): jnp.einsum('fkn,fnd->kfd', left_re, right_re, preferred_element_type=jnp....  9.32 us
  transfers between devices with their start and end apart: 3, of which 3 were waited for; matrix products, arithmetic and copies ran while one was open for 1% of the time, Pallas kernels for 0%

commit v1 on v0

--- a/solution.py
+++ b/solution.py
@@ -38,7 +38,9 @@
     amplitudes = lax.all_to_all(by_dirs, "node", split_axis=0, concat_axis=3, tiled=True)
     colset = lax.all_gather(amplitudes[None], ("node", "drow"), axis=0, tiled=True)
     col_cat = jnp.concatenate([colset[:, :, 0], colset[:, :, 1]], axis=-1)
-    row_piece = lax.all_gather(amplitudes, "dcol", axis=0, tiled=True)
+    row_piece = jnp.concatenate(
+        lax.all_to_all(jnp.stack([amplitudes] * lax.axis_size("dcol")), "dcol", 0, 0), axis=0
+    )
     lead_re = jnp.concatenate([row_piece[:, 0], row_piece[:, 1]], axis=-1)
     lead_im = jnp.concatenate([row_piece[:, 1], -row_piece[:, 0]], axis=-1)
     spec_re = jnp.einsum("kfe,gsfe->fkgs", lead_re, col_cat, preferred_element_type=jnp.float32)

time: 402 us -> 368 us (0.915)
  waiting for transfers between devices: 222 us -> 122 us
  blocking collectives: 14.2 us -> 79 us
    all_gather x1 -> x0, waiting for transfers between devices: 73.6 us -> none  [local(): row_piece = lax.all_gather(amplitudes, 'dcol', axis=0, tiled=True)]
    all_to_all x0 -> x1, blocking collectives: none -> 64.8 us  [local(): lax.all_to_all(jnp.stack([amplitudes] * lax.axis_size('dcol')), 'dcol', 0...]
    all_gather x1, waiting for transfers between devices: 91.3 us -> 65 us  [local(): lax.all_gather(amplitudes[None], ('node', 'drow'), axis=0, tiled=True)]
  transfers between devices with their start and end apart: 3 -> 2, of which waited for: 3 -> 2; matrix products, arithmetic and copies ran while one was open for 1% -> 0% of each run, Pallas kernels for 0% -> 0%
where the time goes in v1:
time: 368 us; the launch traced here: 364 us
  waiting for transfers between devices  122 us (33%)
  other arithmetic  87.1 us (24%)
  blocking collectives  79 us (21%)
  matrix products  33.2 us (9%)
  local copies, waits for them, and re-layouts  28.9 us (8%)
  between operations  13.6 us (4%)
    convert_element_type x1, other arithmetic, excitation(): load_im = (-spread * jnp.sin(phase_angle)).astype(jnp.bfloat16)  71 us
    all_gather x1, waiting for transfers between devices, local(): lax.all_gather(amplitudes[None], ('node', 'drow'), axis=0, tiled=True)  65 us
    all_to_all x1, blocking collectives, local(): lax.all_to_all(jnp.stack([amplitudes] * lax.axis_size('dcol')), 'dcol', 0...  64.8 us
    reduce_scatter x1, waiting for transfers between devices, local(): lax.psum_scatter(partial_amp, 'node', scatter_dimension=3, tiled=True)  56.8 us
    all_to_all x1, blocking collectives, local(): lax.all_to_all(by_dirs, 'node', split_axis=0, concat_axis=3, tiled=True)  14.2 us
    squeeze x1, local copies, waits for them, and re-layouts, local(): col_cat = jnp.concatenate([colset[:, :, 0], colset[:, :, 1]], axis=-1)  11.6 us
    dot_general x1, matrix products, local(): jnp.einsum('kfe,gsfe->fkgs', lead_re, col_cat, preferred_element_type=jnp...  10 us
    dot_general x1, matrix products, local(): jnp.einsum('fkn,fnd->kfd', left_re, right_re, preferred_element_type=jnp....  9.35 us
  transfers between devices with their start and end apart: 2, of which 2 were waited for; matrix products, arithmetic and copies ran while one was open for 0% of the time, Pallas kernels for 0%

profile of v1, /device:TPU:1, one launch (start us, length us, event | category | flops | bytes accessed | tf_op | source)
XLA Modules:
  0.0 363.6 jit_solution(6154898271901964374)
XLA Ops:
  6.5 0.0 reduce-scatter.2.cloned.1.call-start
  6.5 0.0 copy-start
  6.5 0.0 copy-start.4
  6.5 2.8 slice_bitcast_fusion
  9.4 0.6 copy-done
  10.0 0.0 copy-start.5
  10.0 0.0 copy-start.3
  10.0 0.1 fusion.33
  10.1 0.0 copy-done.4
  10.2 0.5 copy-done.5
  10.7 0.0 copy-done.3
  10.7 0.4 multiply_add_fusion
  11.1 71.0 %multiply_convert_fusion = (bf16[8,1024,512]{1,2,0:T(8,128)(2,1)}, bf16[8,1024,512]{1,2,0:T(8,128)(2,1)}) fusion(f32[8,512]{1,0:T(8,128)S(1)} %get-tuple-element.13, s32[1024,512]{0,1:T(8,128)S(1)} %multiply_add_fusion, s32[8]{0:T(128)S(1)} %iota_add_fusion, f32[8,512]{1,0:T(8,128)S(1)} %get-tuple-element.14), kind=kLoop, calls=%fused_computation.16 | loop fusion | flops 75497472 | bytes 18907168 | tf_op jit(solution)/shard_map/convert_element_type | solution.py:22
  82.1 9.2 %fusion.21 = f32[128,1,8,512]{0,3,2,1:T(8,128)} fusion(bf16[8,128,1024]{2,1,0:T(8,128)(2,1)S(1)} %get-tuple-element.8, bf16[8,128,1024]{2,1,0:T(8,128)(2,1)S(1)} %get-tuple-element.7, bf16[8,1024,512]{1,2,0:T(8,128)(2,1)} %get-tuple-element.10, bf16[8,1024,512]{1,2,0:T(8,128)(2,1)} %get-tuple-element.9), kind=kOutput, calls=%fused_computation.40 | convolution fusion | flops 2189426688 | bytes 23068672 | tf_op jit(solution)/shard_map/fkn,fnd->kfd/dot_general | solution.py:33
  91.3 0.0 copy-start.2
  91.3 9.4 %fusion.24 = f32[128,1,8,512]{0,3,2,1:T(8,128)} fusion(bf16[8,128,1024]{2,1,0:T(8,128)(2,1)S(1)} %get-tuple-element.8, bf16[8,128,1024]{2,1,0:T(8,128)(2,1)S(1)} %fusion.33, bf16[8,1024,512]{1,2,0:T(8,128)(2,1)} %get-tuple-element.9, bf16[8,1024,512]{1,2,0:T(8,128)(2,1)} %get-tuple-element.10), kind=kOutput, calls=%fused_computation.41 | convolution fusion | flops 2189426688 | bytes 23068672 | tf_op jit(solution)/shard_map/fkn,fnd->kfd/dot_general | solution.py:32
  100.7 0.0 copy-done.2
  100.7 3.9 %pad_maximum_fusion.5 = f32[128,2,8,512]{0,3,2,1:T(8,128)} fusion(f32[128,1,8,512]{0,3,2,1:T(8,128)S(1)} %copy-done.2, f32[128,1,8,512]{0,3,2,1:T(8,128)} %fusion.24), kind=kLoop, calls=%fused_computation.27 | loop fusion | flops 1048576 | bytes 8388608 | tf_op jit(solution)/shard_map/stack | solution.py:34
  104.6 0.0 reduce-scatter.2.cloned.1.call-update
  104.6 0.0 all-gather.2.cloned.1.call-start
  104.7 56.8 %reduce-scatter.2.cloned.1.call-done = f32[128,2,8,64]{0,3,2,1:T(8,128)} async-done(((f32[128,2,8,512]{0,3,2,1:T(8,128)}), f32[128,2,8,64]{0,3,2,1:T(8,128)}) %reduce-scatter.2.cloned.1.call-update) | async-done | bytes 524304 | tf_op jit(solution)/shard_map/reduce_scatter | solution.py:35
  161.4 1.1 convert_element_type.19
  162.5 0.4 copy.14
  163.0 0.4 reshape.78
  163.4 14.2 %all_to_all.20 = bf16[8,2,8192]{2,1,0:T(2,128)(2,1)S(1)} all-to-all(bf16[8,2,8192]{2,1,0:T(2,128)(2,1)S(1)} %reshape.78), channel_id=1, replica_groups=mesh['node'=8,'drow'=4,'dcol'=8] {'node'}, dimensions={0} | all-to-all | bytes 524288 | tf_op jit(solution)/shard_map/all_to_all | solution.py:38
  177.6 0.3 reshape.79
  177.9 0.6 copy.15
  178.5 1.0 stack.32
  179.6 0.0 all-gather.2.cloned.1.call-update
  179.6 0.3 copy.29
  179.9 0.3 reshape.77
  180.3 0.3 stack.31
  180.5 64.8 %all_to_all.21 = bf16[8,16,2,8,512]{4,1,3,2,0:T(8,128)(2,1)S(1)} all-to-all(bf16[8,16,2,8,512]{4,1,3,2,0:T(8,128)(2,1)S(1)} %stack.31), channel_id=1, replica_groups=mesh['node'=8,'drow'=4,'dcol'=8] {'dcol'}, dimensions={0} | all-to-all | bytes 4194304 | tf_op jit(solution)/shard_map/all_to_all | solution.py:42
  245.3 0.2 copy.17
  245.6 0.1 fusion.32
  245.6 0.2 slice_bitcast_fusion.3
  245.9 65.0 %all-gather.2.cloned.1.call-done = bf16[32,16,2,8,512]{4,3,2,1,0:T(8,128)(2,1)} async-done(((bf16[1,16,2,8,512]{4,3,2,1,0:T(8,128)(2,1)}), bf16[32,16,2,8,512]{4,3,2,1,0:T(8,128)(2,1)}) %all-gather.2.cloned.1.call-update) | async-done | bytes 8388624 | tf_op jit(solution)/shard_map/all_gather | solution.py:39
  310.9 3.8 %fusion.34 = (bf16[32,16,1,8,512]{4,3,2,1,0:T(8,128)(2,1)S(1)}, bf16[32,16,1,8,512]{4,3,2,1,0:T(8,128)(2,1)S(1)}) fusion(bf16[32,16,2,8,512]{4,3,2,1,0:T(8,128)(2,1)} %all-gather.2.cloned.1.call-done), kind=kLoop, calls=%fused_computation.53 | loop fusion | bytes 16777216 | tf_op jit(solution)/shard_map/slice | solution.py:40
  314.7 11.6 %copy_bitcast_fusion = (bf16[32,16,8,512]{3,0,1,2:T(8,128)(2,1)}, bf16[32,16,8,512]{3,0,1,2:T(8,128)(2,1)}) fusion(bf16[32,16,1,8,512]{4,3,2,1,0:T(8,128)(2,1)S(1)} %get-tuple-element.6, bf16[32,16,1,8,512]{4,3,2,1,0:T(8,128)(2,1)S(1)} %get-tuple-element.5), kind=kLoop, calls=%fused_computation.29 | loop fusion | bytes 16777216 | tf_op jit(solution)/shard_map/squeeze | solution.py:40
  326.3 8.2 %pad_maximum_fusion = bf16[32,16,8,1024]{3,0,1,2:T(8,128)(2,1)} fusion(bf16[32,16,8,512]{3,0,1,2:T(8,128)(2,1)} %get-tuple-element.19, bf16[32,16,8,512]{3,0,1,2:T(8,128)(2,1)} %get-tuple-element.20), kind=kLoop, calls=%fused_computation.18 | loop fusion | flops 16777216 | bytes 16777216 | tf_op jit(solution)/shard_map/concatenate | solution.py:40
  334.5 0.0 copy-start.1
  334.5 10.0 %fusion.13 = f32[8,128,32,16]{1,3,2,0:T(8,128)S(1)} fusion(bf16[32,16,8,1024]{3,0,1,2:T(8,128)(2,1)} %pad_maximum_fusion, bf16[128,8,512]{2,0,1:T(8,128)(2,1)S(1)} %get-tuple-element.12, bf16[128,8,512]{2,0,1:T(8,128)(2,1)S(1)} %get-tuple-element.11), kind=kOutput, calls=%fused_computation.21 | convolution fusion | flops 1077936128 | bytes 12582912 | tf_op jit(solution)/shard_map/kfe,gsfe->fkgs/dot_general | solution.py:46
  344.5 0.0 copy-done.1
  344.5 4.6 %fusion.11 = f32[8,128,32,16]{1,3,2,0:T(8,128)S(1)} fusion(bf16[32,16,8,1024]{3,0,1,2:T(8,128)(2,1)S(1)} %copy-done.1, bf16[128,8,512]{2,0,1:T(8,128)(2,1)S(1)} %fusion.32, bf16[128,8,512]{2,0,1:T(8,128)(2,1)S(1)} %get-tuple-element.12), kind=kOutput, calls=%fused_computation.19 | convolution fusion | flops 1077936128 | bytes 12582912 | tf_op jit(solution)/shard_map/kfe,gsfe->fkgs/dot_general | solution.py:47
  349.2 2.3 maximum_bitcast_fusion
  351.5 5.3 %copy.23 = f32[2,8,1,128,512]{4,3,2,1,0:T(8,128)} copy(f32[2,8,1,128,512]{3,4,1,0,2:T(8,128)} %maximum_bitcast_fusion) | data formatting | bytes 8388608 | tf_op jit(solution)/shard_map/broadcast_in_dim | solution.py:51
  (4 shorter events, 0.0 us)
Async XLA Ops:
  6.5 154.9 %reduce-scatter.2.cloned.1.call-start = ((), (), s32[]{:S(2)}) async-start(), calls=%async_computation.3 | async-start | bytes 4718592 | tf_op jit(solution)/shard_map/reduce_scatter | solution.py:35
  6.5 3.4 copy-start
  6.5 3.6 copy-start.4
  10.0 0.7 copy-start.5
  10.0 0.7 copy-start.3
  91.3 9.4 %copy-start.2 = (f32[128,1,8,512]{0,3,2,1:T(8,128)S(1)}, f32[128,1,8,512]{0,3,2,1:T(8,128)}, u32[]{:S(2)}) copy-start(f32[128,1,8,512]{0,3,2,1:T(8,128)} %fusion.21) | copy-start | bytes 6291460
  104.6 206.3 %all-gather.2.cloned.1.call-start = ((), (), s32[]{:S(2)}) async-start(), calls=%async_computation.4 | async-start | bytes 8650752 | tf_op jit(solution)/shard_map/all_gather | solution.py:39
  334.5 10.1 %copy-start.1 = (bf16[32,16,8,1024]{3,0,1,2:T(8,128)(2,1)S(1)}, bf16[32,16,8,1024]{3,0,1,2:T(8,128)(2,1)}, u32[]{:S(2)}) copy-start(bf16[32,16,8,1024]{3,0,1,2:T(8,128)(2,1)} %pad_maximum_fusion) | copy-start | bytes 25165828
Sparse Core Ops, SparseCore 0:
  104.7 56.6 reduce-scatter.1
  179.7 131.1 all-gather.1
